TPU v7x, 512 devices: a whole 4x4x16 slice. The times are simulated.
512 devices in a mesh: rows: 64 (over x_hi, z, core), chan: 8 (over x_lo, y).
Axes of the slice: x: 4 (x_hi: 2, x_lo: 2; x = x_hi * 2 + x_lo), y: 4, z: 16, core: 2. Of those that a mesh axis runs over, the one named last changes fastest.
Arguments:
- hidden: float32 [32, 2048, 2048], P('chan', 'rows'), may hold values from -6 to 6
- front: float32 [2048, 2048], P('rows', 'chan'), may hold values from -6 to 6
- spectral_weight: float32 [2, 128, 128, 32, 32], P(None, 'rows', 'chan'), may hold values from -0.5 to 0.5
- skip_gain: float32 [32], P('chan'), may hold values from 0.5 to 1.5
- skip_bias: float32 [32], P('chan'), may hold values from -3 to 3
- project_weight: float32 [2, 32], P(None, 'chan'), may hold values from -1 to 1
- project_bias: float32 [2], replicated, may hold values from -3 to 3
- ice_mask: int32 [2048, 2048], P('rows', 'chan'), may hold values 0 or 1
- front_flags: int32 [2048, 2048], P('rows', 'chan'), may hold values 0 or 1
Outputs:
- velocity: float32 [2, 2048, 2048], P(None, 'rows', 'chan')
- front_next: float32 [2048, 2048], P('rows', 'chan')
All inputs are finite; a program needn't handle non-finite values. No bound on the sum of `ice_mask` or of `front_flags` on one device may be relied on, other than what follows from the above.
Results may differ from a plain program's by a relative error of at most 0.0003.
Values sent between devices are 32-bit elements; how exact they have to be, the bound alone decides.
No kernel may reach another device: no remote copies, remote signals or barrier semaphores. Data moves between devices by JAX's collectives and lax.ppermute only.
A program may use at most 128 MiB of HBM per device.

v0:
```python
import math
import jax
import jax.numpy as jnp
from jax import lax
from jax.sharding import PartitionSpec as P

LS_STEPS = 4
time_step = 0.25
highest = lax.Precision.HIGHEST


def with_halo(block, sides, width):
    for axis, dim in sides:
        count = lax.axis_size(axis)
        forward = [(i, i + 1) for i in range(count - 1)]
        backward = [(target, source) for source, target in forward]
        low = lax.ppermute(
            lax.slice_in_dim(block, block.shape[dim] - width, None, axis=dim), axis, forward
        )
        high = lax.ppermute(lax.slice_in_dim(block, 0, width, axis=dim), axis, backward)
        block = jnp.concatenate([low, block, high], axis=dim)
    return block


def angles(freqs, places, length):
    product = freqs[:, None] * places[None, :] % length
    return 2.0 * math.pi / length * product.astype(jnp.float32)


def x_tables(total_modes, places, length):
    mode_ids = jnp.arange(total_modes, dtype=jnp.int32)
    wave_ids = mode_ids - total_modes * (mode_ids >= total_modes // 2).astype(jnp.int32)
    phase = angles(wave_ids, places, length)
    return jnp.stack([jnp.cos(phase), jnp.sin(phase)])


def forward_x(spectra, tables):
    parts = jnp.einsum("cqrx,spx->cqrsp", spectra, tables, precision=highest)
    real_part = parts[:, :, 0, 0] + parts[:, :, 1, 1]
    imag_part = parts[:, :, 1, 0] - parts[:, :, 0, 1]
    return jnp.stack([real_part, imag_part], axis=2)


def inverse_x(spectra, tables):
    parts = jnp.einsum("cqrp,spx->cqrsx", spectra, tables, precision=highest)
    real_part = parts[:, :, 0, 0] - parts[:, :, 1, 1]
    imag_part = parts[:, :, 0, 1] + parts[:, :, 1, 0]
    stacked = jnp.stack([real_part, imag_part], axis=2)
    return stacked.reshape(stacked.shape[0], stacked.shape[1] * 2, stacked.shape[3])


def advance(padded, speed_x, speed_y, band):
    center = padded[1:-1, 1:-1]
    back_x = center - padded[:-2, 1:-1]
    ahead_x = padded[2:, 1:-1] - center
    back_y = center - padded[1:-1, :-2]
    ahead_y = padded[1:-1, 2:] - center
    transport = jnp.maximum(speed_x, 0.0) * back_x + jnp.minimum(speed_x, 0.0) * ahead_x
    transport = transport + jnp.maximum(speed_y, 0.0) * back_y + jnp.minimum(speed_y, 0.0) * ahead_y
    return center - time_step * band * transport


def on_device(
    hidden,
    front,
    spectral_weight,
    skip_gain,
    skip_bias,
    project_weight,
    project_bias,
    ice_mask,
    front_flags,
):
    local_chan, row_count, columns = hidden.shape
    row_devices = lax.axis_size("rows")
    chan_devices = lax.axis_size("chan")
    local_ymodes = spectral_weight.shape[1]
    all_rows = row_count * row_devices
    all_xmodes = spectral_weight.shape[2] * chan_devices
    all_ymodes = local_ymodes * row_devices
    norm_scale = 1.0 / math.sqrt(all_rows * columns * all_xmodes * all_ymodes)
    y_ids = jnp.arange(all_ymodes, dtype=jnp.int32)
    y_phase = angles(y_ids, jnp.arange(columns, dtype=jnp.int32), columns)
    forward_y = jnp.stack([jnp.cos(y_phase), -jnp.sin(y_phase)], axis=1).reshape(
        2 * all_ymodes, columns
    )
    y_weights = jnp.where(y_ids == 0, 1.0, 2.0).astype(jnp.float32)[:, None] * norm_scale
    inverse_y = jnp.stack(
        [y_weights * jnp.cos(y_phase), -y_weights * jnp.sin(y_phase)], axis=1
    ).reshape(2 * all_ymodes, columns)
    spec_y = jnp.einsum("cxy,ky->ckx", hidden, forward_y, precision=highest)
    own_rows = lax.axis_index("rows") * row_count + jnp.arange(row_count, dtype=jnp.int32)
    local_tables = x_tables(all_xmodes, own_rows, all_rows)
    picked = spec_y
    picked = picked.reshape(local_chan, local_ymodes * lax.axis_size("rows"), 2, row_count)
    owned = lax.psum_scatter(
        jnp.transpose(forward_x(picked, local_tables), (1, 0, 2, 3)),
        "rows",
        scatter_dimension=0,
        tiled=True,
    )
    spectra = jnp.transpose(owned, (1, 0, 2, 3))
    gathered = lax.all_to_all(spectra, "chan", split_axis=3, concat_axis=0, tiled=True)
    real_in = gathered[:, :, 0]
    imag_in = gathered[:, :, 1]
    real_out = jnp.einsum(
        "qpio,iqp->oqp", spectral_weight[0], real_in, precision=highest
    ) - jnp.einsum("qpio,iqp->oqp", spectral_weight[1], imag_in, precision=highest)
    imag_out = jnp.einsum(
        "qpio,iqp->oqp", spectral_weight[0], imag_in, precision=highest
    ) + jnp.einsum("qpio,iqp->oqp", spectral_weight[1], real_in, precision=highest)
    mixed = lax.all_to_all(
        jnp.stack([real_out, imag_out], axis=2), "chan", split_axis=0, concat_axis=3, tiled=True
    )
    inverted = inverse_x(lax.all_gather(mixed, "rows", axis=1, tiled=True), local_tables)
    spectral = jnp.einsum("ckx,ky->cxy", inverted, inverse_y, precision=highest)
    activated = jax.nn.gelu(
        spectral + skip_gain[:, None, None] * hidden + skip_bias[:, None, None], approximate=False
    )
    partial_speed = jnp.einsum("jc,cxy->jxy", project_weight, activated, precision=highest)
    tile_speed = (
        lax.psum_scatter(partial_speed, "chan", scatter_dimension=2, tiled=True)
        + project_bias[:, None, None]
    )
    velocity = tile_speed * ice_mask.astype(jnp.float32)[None]
    band = front_flags.astype(jnp.float32)
    level = front
    for level_step in range(LS_STEPS):
        padded = with_halo(level, (("rows", 0), ("chan", 1)), 1)
        level = advance(padded, velocity[0], velocity[1], band)
    return (velocity, level)


def solution(mesh):
    return jax.shard_map(
        on_device,
        mesh=mesh,
        in_specs=(
            P("chan", "rows", None),
            P("rows", "chan"),
            P(None, "rows", "chan", None, None),
            P("chan"),
            P("chan"),
            P(None, "chan"),
            P(),
            P("rows", "chan"),
            P("rows", "chan"),
        ),
        out_specs=(P(None, "rows", "chan"), P("rows", "chan")),
        check_vma=False,
    )
```

profile of v0, /device:TPU:28, one launch (start us, length us, event | category | flops | bytes accessed | tf_op | source)
XLA Modules:
  0.0 833.2 jit_solution(7316440260785637963)
XLA Ops:
  7.2 4.1 fusion.29
  15.7 3.8 convolution_bitcast_fusion.2
  24.0 527.4 %all-reduce.3.cloned.1.call-done = f32[128,4,2,128]{3,1,2,0:T(4,128)} async-done(((f32[128,4,2,128]{3,1,2,0:T(4,128)}), f32[128,4,2,128]{3,1,2,0:T(4,128)}) %all-reduce.3.cloned.1.call-update) | async-done | bytes 524304
  553.3 5.4 all-to-all-start
  558.7 4.1 all-to-all-done
  566.6 5.3 all-to-all-start.1
  572.0 4.2 broadcast_multiply_fusion
  577.2 76.0 %all_gather.3 = f32[4,128,2,128]{3,0,2,1:T(4,128)S(1)} all-gather(f32[4,2,2,128]{3,0,2,1:T(4,128)S(1)} %reshape.387), channel_id=1, replica_groups=mesh['rows'=64,'chan'=8] {'rows'}, dimensions={1}, use_global_device_ids=true | all-gather | bytes 532480 | tf_op jit(solution)/shard_map/all_gather | solution.py:115
  660.0 26.2 %copy.126 = f32[2,32,2048]{0,1,2:T(8,128)} copy(f32[2,32,2048]{2,0,1:T(2,128)S(1)} %convolution_bitcast_fusion.1) | data formatting | bytes 1048576
  686.2 28.6 %reshape.388 = f32[2048,64]{1,0:T(8,128)} reshape(f32[2048,32,2]{2,1,0:T(8,128)} %bitcast.135) | data formatting | bytes 1048576
  717.0 6.9 collective-permute-start.1
  725.3 4.4 collective-permute-start.2
  731.9 19.4 %reduce-scatter.4.cloned.1.call-done = f32[256,64]{1,0:T(8,128)} async-done(((f32[2048,64]{1,0:T(8,128)}), f32[256,64]{1,0:T(8,128)}) %reduce-scatter.4.cloned.1.call-update) | async-done | bytes 65552
  751.4 6.5 reshape.389
  757.8 3.6 copy.127
  763.7 7.3 collective-permute-start.5
  772.3 4.8 collective-permute-start.6
  779.1 5.8 collective-permute-done.7
  787.0 7.3 collective-permute-start.9
  797.5 3.9 collective-permute-start.11
  801.5 3.8 collective-permute-done.11
  807.4 7.3 collective-permute-start.13
  817.9 3.9 collective-permute-start.15
  821.8 3.8 collective-permute-done.15
  (110 shorter events, 44.0 us)
Async XLA Ops:
  7.2 650.3 %copy-start = (f32[2,4]{1,0:T(2,128)S(1)}, f32[2,4]{1,0:T(2,128)}, u32[]{:S(2)}) copy-start(f32[2,4]{1,0:T(2,128)} %param.14) | copy-start | bytes 100
  7.2 544.3 %all-reduce.3.cloned.1.call-start = ((), (), s32[]{:S(2)}) async-start(), calls=%async_computation.4 | async-start | bytes 1048576
  20.9 544.0 %copy-start.2 = (f32[2,2,16,32,32]{4,3,2,1,0:T(8,128)S(1)}, f32[2,2,16,32,32]{4,3,2,1,0:T(8,128)}, u32[]{:S(2)}) copy-start(f32[2,2,16,32,32]{4,3,2,1,0:T(8,128)} %param.11) | copy-start | bytes 786436
  553.3 9.5 %all-to-all-start = ((f32[8,1,256]{2,1,0:T(1,128)}), f32[8,1,256]{2,1,0:T(1,128)S(1)}, u32[]{:S(2)}, u32[]{:S(2)}) async-start(f32[8,1,256]{2,1,0:T(1,128)} %reshape.391), calls=%async_computation | async-start | bytes 16384 | tf_op jit(solution)/shard_map/all_to_all | solution.py:103
  566.6 9.6 %all-to-all-start.1 = ((f32[8,1,256]{2,1,0:T(1,128)}), f32[8,1,256]{2,1,0:T(1,128)S(1)}, u32[]{:S(2)}, u32[]{:S(2)}) async-start(f32[8,1,256]{2,1,0:T(1,128)} %reshape.393), calls=%async_computation.1 | async-start | bytes 16384 | tf_op jit(solution)/shard_map/all_to_all | solution.py:112
  572.0 82.0 %copy-start.8 = (f32[4]{0:T(128)S(1)}, f32[4]{0:T(128)}, u32[]{:S(2)}) copy-start(f32[4]{0:T(128)} %param.13) | copy-start | bytes 52
  572.0 82.0 %copy-start.9 = (f32[4]{0:T(128)S(1)}, f32[4]{0:T(128)}, u32[]{:S(2)}) copy-start(f32[4]{0:T(128)} %param.12) | copy-start | bytes 52
  572.0 179.4 %reduce-scatter.4.cloned.1.call-start = ((), (), s32[]{:S(2)}) async-start(), calls=%async_computation.3 | async-start | bytes 1179648
  714.8 9.2 %collective-permute-start = (f32[1,256]{1,0:T(1,128)S(1)}, f32[1,256]{1,0:T(1,128)S(1)}, u32[]{:S(2)}, u32[]{:S(2)}) collective-permute-start(f32[1,256]{1,0:T(1,128)S(1)} %get-tuple-element.36), channel_id=1, source_target_pairs={{0,8},{8,16},{16,24},{24,32},{32,40},{40,48},{48,56},{56,64},{64,7... | collective-permute-start | bytes 3080 | tf_op jit(solution)/shard_map/ppermute | solution.py:17
  717.0 8.2 collective-permute-start.1
  725.3 36.3 %collective-permute-start.2 = (f32[34,1]{1,0:T(8,128)S(1)}, f32[34,1]{1,0:T(8,128)S(1)}, u32[]{:S(2)}, u32[]{:S(2)}) collective-permute-start(f32[34,1]{1,0:T(8,128)S(1)} %get-tuple-element.28), channel_id=1, source_target_pairs={{0,1},{1,2},{2,3},{3,4},{4,5},{5,6},{6,7},{8,9},{9,10},{10,11},{11... | collective-permute-start | bytes 416 | tf_op jit(solution)/shard_map/ppermute | solution.py:17
  729.8 31.9 %collective-permute-start.3 = (f32[34,1]{1,0:T(8,128)S(1)}, f32[34,1]{1,0:T(8,128)S(1)}, u32[]{:S(2)}, u32[]{:S(2)}) collective-permute-start(f32[34,1]{1,0:T(8,128)S(1)} %get-tuple-element.29), channel_id=1, source_target_pairs={{1,0},{2,1},{3,2},{4,3},{5,4},{6,5},{7,6},{9,8},{10,9},{11,10},{12... | collective-permute-start | bytes 416 | tf_op jit(solution)/shard_map/ppermute | solution.py:20
  761.8 9.2 %collective-permute-start.4 = (f32[1,256]{1,0:T(1,128)S(1)}, f32[1,256]{1,0:T(1,128)S(1)}, u32[]{:S(2)}, u32[]{:S(2)}) collective-permute-start(f32[1,256]{1,0:T(1,128)S(1)} %get-tuple-element.34), channel_id=1, source_target_pairs={{0,8},{8,16},{16,24},{24,32},{32,40},{40,48},{48,56},{56,64},{64,7... | collective-permute-start | bytes 3080 | tf_op jit(solution)/shard_map/ppermute | solution.py:17
  763.7 8.5 %collective-permute-start.5 = (f32[1,256]{1,0:T(1,128)S(1)}, f32[1,256]{1,0:T(1,128)S(1)}, u32[]{:S(2)}, u32[]{:S(2)}) collective-permute-start(f32[1,256]{1,0:T(1,128)S(1)} %get-tuple-element.35), channel_id=1, source_target_pairs={{8,0},{16,8},{24,16},{32,24},{40,32},{48,40},{56,48},{64,56},{72,6... | collective-permute-start | bytes 3080 | tf_op jit(solution)/shard_map/ppermute | solution.py:20
  772.3 6.7 collective-permute-start.6
  777.2 7.8 collective-permute-start.7
  785.1 9.2 %collective-permute-start.8 = (f32[1,256]{1,0:T(1,128)S(1)}, f32[1,256]{1,0:T(1,128)S(1)}, u32[]{:S(2)}, u32[]{:S(2)}) collective-permute-start(f32[1,256]{1,0:T(1,128)S(1)} %get-tuple-element.32), channel_id=1, source_target_pairs={{0,8},{8,16},{16,24},{24,32},{32,40},{40,48},{48,56},{56,64},{64,7... | collective-permute-start | bytes 3080 | tf_op jit(solution)/shard_map/ppermute | solution.py:17
  787.0 8.5 %collective-permute-start.9 = (f32[1,256]{1,0:T(1,128)S(1)}, f32[1,256]{1,0:T(1,128)S(1)}, u32[]{:S(2)}, u32[]{:S(2)}) collective-permute-start(f32[1,256]{1,0:T(1,128)S(1)} %get-tuple-element.33), channel_id=1, source_target_pairs={{8,0},{16,8},{24,16},{32,24},{40,32},{48,40},{56,48},{64,56},{72,6... | collective-permute-start | bytes 3080 | tf_op jit(solution)/shard_map/ppermute | solution.py:20
  795.6 5.9 collective-permute-start.10
  797.5 7.8 collective-permute-start.11
  805.4 9.2 %collective-permute-start.12 = (f32[1,256]{1,0:T(1,128)S(1)}, f32[1,256]{1,0:T(1,128)S(1)}, u32[]{:S(2)}, u32[]{:S(2)}) collective-permute-start(f32[1,256]{1,0:T(1,128)S(1)} %get-tuple-element.30), channel_id=1, source_target_pairs={{0,8},{8,16},{16,24},{24,32},{32,40},{40,48},{48,56},{56,64},{64,7... | collective-permute-start | bytes 3080 | tf_op jit(solution)/shard_map/ppermute | solution.py:17
  807.4 8.5 %collective-permute-start.13 = (f32[1,256]{1,0:T(1,128)S(1)}, f32[1,256]{1,0:T(1,128)S(1)}, u32[]{:S(2)}, u32[]{:S(2)}) collective-permute-start(f32[1,256]{1,0:T(1,128)S(1)} %get-tuple-element.31), channel_id=1, source_target_pairs={{8,0},{16,8},{24,16},{32,24},{40,32},{48,40},{56,48},{64,56},{72,6... | collective-permute-start | bytes 3080 | tf_op jit(solution)/shard_map/ppermute | solution.py:20
  816.0 5.9 collective-permute-start.14
  817.9 7.8 collective-permute-start.15
  (6 other events, 141.1 us)
Sparse Core Ops, SparseCore 0:
  22.2 529.1 all-reduce.2
  714.9 36.4 reduce-scatter.3
where the time goes:
time: 834 us; the launch traced here: 833 us
  waiting for transfers between devices  570 us (68%)
  local copies, waits for them, and re-layouts  76.4 us (9%)
  blocking collectives  76 us (9%)
  starting transfers between devices  72.4 us (9%)
  between operations  15.3 us (2%)
  other arithmetic  12 us (1%)
  matrix products  11.5 us (1%)
    unnamed x4, waiting for transfers between devices  547 us
    all_gather x1, blocking collectives, on_device(): lax.all_gather(mixed, 'rows', axis=1, tiled=True)  76 us
    unnamed x33, local copies, waits for them, and re-layouts  68.5 us
    ppermute x8, starting transfers between devices, with_halo(): lax.ppermute(lax.slice_in_dim(block, 0, width, axis=dim), axis, backward)  40.6 us
    ppermute x8, starting transfers between devices, with_halo(): lax.ppermute(lax.slice_in_dim(block, block.shape[dim] - width, None, axis...  21.1 us
    ppermute x8, waiting for transfers between devices, with_halo(): lax.ppermute(lax.slice_in_dim(block, 0, width, axis=dim), axis, backward)  18.6 us
  transfers between devices with their start and end apart: 20, of which 10 were waited for; matrix products, arithmetic and copies ran while one was open for 2% of the time, Pallas kernels for 0%

commit v1 on v0

--- a/solution.py
+++ b/solution.py
@@ -7,6 +7,14 @@
 LS_STEPS = 4
 time_step = 0.25
 highest = lax.Precision.HIGHEST
+
+
+def create_the_streams(chunk, dim_i):
+    reached = jnp.concatenate(
+        lax.all_to_all(jnp.stack([chunk for _ in range(lax.axis_size("rows"))]), "rows", 0, 0),
+        axis=dim_i,
+    )
+    return reached
 
 
 def with_halo(block, sides, width):
@@ -112,7 +120,7 @@
     mixed = lax.all_to_all(
         jnp.stack([real_out, imag_out], axis=2), "chan", split_axis=0, concat_axis=3, tiled=True
     )
-    inverted = inverse_x(lax.all_gather(mixed, "rows", axis=1, tiled=True), local_tables)
+    inverted = inverse_x(create_the_streams(mixed, 1), local_tables)
     spectral = jnp.einsum("ckx,ky->cxy", inverted, inverse_y, precision=highest)
     activated = jax.nn.gelu(
         spectral + skip_gain[:, None, None] * hidden + skip_bias[:, None, None], approximate=False

time: 834 us -> 799 us (0.958)
  blocking collectives: 76 us -> 17.9 us
  waiting for transfers between devices: 570 us -> 593 us
    all_gather x1 -> x0, blocking collectives: 76 us -> none  [on_device(): lax.all_gather(mixed, 'rows', axis=1, tiled=True)]
    all_to_all x2 -> x1, waiting for transfers between devices: 4.13 us -> 23.8 us  [create_the_streams(): lax.all_to_all(jnp.stack([chunk for _ in range(lax.axis_size('rows'))]),...]
    all_to_all x0 -> x2, blocking collectives: none -> 17.9 us  [the longest x1 9.32 us: on_device(): lax.all_to_all(spectra, 'chan', split_axis=3, concat_axis=0, tiled=True)]
    unnamed x33 -> x37, local copies, waits for them, and re-layouts: 68.5 us -> 67.9 us
  transfers between devices with their start and end apart: 20 -> 19, of which waited for: 10 -> 10; matrix products, arithmetic and copies ran while one was open for 2% -> 2% of each run, Pallas kernels for 0% -> 0%
where the time goes in v1:
time: 799 us; the launch traced here: 798 us
  waiting for transfers between devices  593 us (74%)
  local copies, waits for them, and re-layouts  76.9 us (10%)
  starting transfers between devices  69.5 us (9%)
  blocking collectives  17.9 us (2%)
  between operations  15.3 us (2%)
  other arithmetic  13.4 us (2%)
  matrix products  11.4 us (1%)
    unnamed x4, waiting for transfers between devices  551 us
    unnamed x37, local copies, waits for them, and re-layouts  67.9 us
    ppermute x8, starting transfers between devices, with_halo(): lax.ppermute(lax.slice_in_dim(block, 0, width, axis=dim), axis, backward)  40.3 us
    all_to_all x1, waiting for transfers between devices, create_the_streams(): lax.all_to_all(jnp.stack([chunk for _ in range(lax.axis_size('rows'))]),...  23.8 us
    ppermute x8, starting transfers between devices, with_halo(): lax.ppermute(lax.slice_in_dim(block, block.shape[dim] - width, None, axis...  21.2 us
    ppermute x8, waiting for transfers between devices, with_halo(): lax.ppermute(lax.slice_in_dim(block, 0, width, axis=dim), axis, backward)  18.6 us
  transfers between devices with their start and end apart: 19, of which 10 were waited for; matrix products, arithmetic and copies ran while one was open for 2% of the time, Pallas kernels for 0%

profile of v1, /device:TPU:28, one launch (start us, length us, event | category | flops | bytes accessed | tf_op | source)
XLA Modules:
  0.0 797.5 jit_solution(4239131399082929265)
XLA Ops:
  7.2 4.1 fusion.27
  15.7 3.8 convolution_bitcast_fusion.2
  24.0 527.7 %all-reduce.3.cloned.1.call-done = f32[128,4,2,128]{3,1,2,0:T(4,128)} async-done(((f32[128,4,2,128]{3,1,2,0:T(4,128)}), f32[128,4,2,128]{3,1,2,0:T(4,128)}) %all-reduce.3.cloned.1.call-update) | async-done | bytes 524304
  553.0 9.3 %all_to_all.38 = f32[8,1,256]{2,1,0:T(1,128)S(1)} all-to-all(f32[8,1,256]{2,1,0:T(1,128)S(1)} %reshape.402), channel_id=1, replica_groups=mesh['rows'=64,'chan'=8] {'chan'}, dimensions={0} | all-to-all | bytes 16384 | tf_op jit(solution)/shard_map/all_to_all | solution.py:111
  565.5 8.6 %all_to_all.39 = f32[8,1,256]{2,1,0:T(1,128)S(1)} all-to-all(f32[8,1,256]{2,1,0:T(1,128)S(1)} %reshape.404), channel_id=1, replica_groups=mesh['rows'=64,'chan'=8] {'chan'}, dimensions={0} | all-to-all | bytes 16384 | tf_op jit(solution)/shard_map/all_to_all | solution.py:120
  575.9 7.9 all-to-all-start.2
  584.0 5.6 broadcast_multiply_fusion
  589.5 23.8 %all-to-all-done.2 = f32[64,4,2,2,128]{4,2,3,1,0:T(2,128)S(1)} async-done(((f32[64,4,2,2,128]{4,2,3,1,0:T(2,128)}), f32[64,4,2,2,128]{4,2,3,1,0:T(2,128)S(1)}, u32[]{:S(2)}, u32[]{:S(2)}) %all-to-all-start.2) | async-done | bytes 524320 | tf_op jit(solution)/shard_map/all_to_all | solution.py:14
  620.9 26.2 %copy.121 = f32[2,32,2048]{0,1,2:T(8,128)} copy(f32[2,32,2048]{2,0,1:T(2,128)S(1)} %convolution_bitcast_fusion.1) | data formatting | bytes 1048576
  647.1 28.6 %reshape.399 = f32[2048,64]{1,0:T(8,128)} reshape(f32[2048,32,2]{2,1,0:T(8,128)} %bitcast.141) | data formatting | bytes 1048576
  678.3 6.6 collective-permute-start.1
  686.3 4.0 collective-permute-start.2
  692.4 23.0 %reduce-scatter.4.cloned.1.call-done = f32[256,64]{1,0:T(8,128)} async-done(((f32[2048,64]{1,0:T(8,128)}), f32[256,64]{1,0:T(8,128)}) %reduce-scatter.4.cloned.1.call-update) | async-done | bytes 65552
  715.4 6.5 reshape.400
  721.9 3.6 copy.122
  727.7 7.3 collective-permute-start.5
  736.4 5.1 collective-permute-start.6
  743.4 5.8 collective-permute-done.7
  751.3 7.3 collective-permute-start.9
  761.8 3.9 collective-permute-start.11
  765.8 3.8 collective-permute-done.11
  771.7 7.3 collective-permute-start.13
  782.2 3.9 collective-permute-start.15
  786.1 3.8 collective-permute-done.15
  (115 shorter events, 44.8 us)
Async XLA Ops:
  7.2 611.2 %copy-start = (f32[2,4]{1,0:T(2,128)S(1)}, f32[2,4]{1,0:T(2,128)}, u32[]{:S(2)}) copy-start(f32[2,4]{1,0:T(2,128)} %param.14) | copy-start | bytes 100
  7.2 544.5 %all-reduce.3.cloned.1.call-start = ((), (), s32[]{:S(2)}) async-start(), calls=%async_computation.5 | async-start | bytes 1048576
  20.9 543.5 %copy-start.2 = (f32[2,2,16,32,32]{4,3,2,1,0:T(8,128)S(1)}, f32[2,2,16,32,32]{4,3,2,1,0:T(8,128)}, u32[]{:S(2)}) copy-start(f32[2,2,16,32,32]{4,3,2,1,0:T(8,128)} %param.11) | copy-start | bytes 786436
  575.9 37.4 %all-to-all-start.2 = ((f32[64,4,2,2,128]{4,2,3,1,0:T(2,128)}), f32[64,4,2,2,128]{4,2,3,1,0:T(2,128)S(1)}, u32[]{:S(2)}, u32[]{:S(2)}) async-start(f32[64,4,2,2,128]{4,2,3,1,0:T(2,128)} %stack.27), calls=%async_computation.2 | async-start | bytes 1048576 | tf_op jit(solution)/shard_map/all_to_all | solution.py:14
  583.9 131.5 %reduce-scatter.4.cloned.1.call-start = ((), (), s32[]{:S(2)}) async-start(), calls=%async_computation.4 | async-start | bytes 1179648
  583.9 30.4 %copy-start.10 = (f32[4]{0:T(128)S(1)}, f32[4]{0:T(128)}, u32[]{:S(2)}) copy-start(f32[4]{0:T(128)} %param.13) | copy-start | bytes 52
  647.1 37.8 %copy-start.8 = (s32[32,256]{1,0:T(8,128)S(1)}, s32[32,256]{1,0:T(8,128)}, u32[]{:S(2)}) copy-start(s32[32,256]{1,0:T(8,128)} %param.16) | copy-start | bytes 98308
  675.7 9.2 %collective-permute-start = (f32[1,256]{1,0:T(1,128)S(1)}, f32[1,256]{1,0:T(1,128)S(1)}, u32[]{:S(2)}, u32[]{:S(2)}) collective-permute-start(f32[1,256]{1,0:T(1,128)S(1)} %get-tuple-element.36), channel_id=1, source_target_pairs={{0,8},{8,16},{16,24},{24,32},{32,40},{40,48},{48,56},{56,64},{64,7... | collective-permute-start | bytes 3080 | tf_op jit(solution)/shard_map/ppermute | solution.py:25
  678.3 7.9 collective-permute-start.1
  686.3 39.4 %collective-permute-start.2 = (f32[34,1]{1,0:T(8,128)S(1)}, f32[34,1]{1,0:T(8,128)S(1)}, u32[]{:S(2)}, u32[]{:S(2)}) collective-permute-start(f32[34,1]{1,0:T(8,128)S(1)} %get-tuple-element.28), channel_id=1, source_target_pairs={{0,1},{1,2},{2,3},{3,4},{4,5},{5,6},{6,7},{8,9},{9,10},{10,11},{11... | collective-permute-start | bytes 416 | tf_op jit(solution)/shard_map/ppermute | solution.py:25
  690.3 35.4 %collective-permute-start.3 = (f32[34,1]{1,0:T(8,128)S(1)}, f32[34,1]{1,0:T(8,128)S(1)}, u32[]{:S(2)}, u32[]{:S(2)}) collective-permute-start(f32[34,1]{1,0:T(8,128)S(1)} %get-tuple-element.29), channel_id=1, source_target_pairs={{1,0},{2,1},{3,2},{4,3},{5,4},{6,5},{7,6},{9,8},{10,9},{11,10},{12... | collective-permute-start | bytes 416 | tf_op jit(solution)/shard_map/ppermute | solution.py:28
  725.7 65.1 %copy-start.5 = (f32[2,32,256]{2,1,0:T(8,128)}, f32[2,32,256]{2,1,0:T(8,128)S(1)}, u32[]{:S(2)}) copy-start(f32[2,32,256]{2,1,0:T(8,128)S(1)} %copy.89) | copy-start | bytes 196612
  725.8 9.2 %collective-permute-start.4 = (f32[1,256]{1,0:T(1,128)S(1)}, f32[1,256]{1,0:T(1,128)S(1)}, u32[]{:S(2)}, u32[]{:S(2)}) collective-permute-start(f32[1,256]{1,0:T(1,128)S(1)} %get-tuple-element.34), channel_id=1, source_target_pairs={{0,8},{8,16},{16,24},{24,32},{32,40},{40,48},{48,56},{56,64},{64,7... | collective-permute-start | bytes 3080 | tf_op jit(solution)/shard_map/ppermute | solution.py:25
  727.7 8.5 %collective-permute-start.5 = (f32[1,256]{1,0:T(1,128)S(1)}, f32[1,256]{1,0:T(1,128)S(1)}, u32[]{:S(2)}, u32[]{:S(2)}) collective-permute-start(f32[1,256]{1,0:T(1,128)S(1)} %get-tuple-element.35), channel_id=1, source_target_pairs={{8,0},{16,8},{24,16},{32,24},{40,32},{48,40},{56,48},{64,56},{72,6... | collective-permute-start | bytes 3080 | tf_op jit(solution)/shard_map/ppermute | solution.py:28
  736.4 7.0 collective-permute-start.6
  741.4 7.8 collective-permute-start.7
  749.3 9.2 %collective-permute-start.8 = (f32[1,256]{1,0:T(1,128)S(1)}, f32[1,256]{1,0:T(1,128)S(1)}, u32[]{:S(2)}, u32[]{:S(2)}) collective-permute-start(f32[1,256]{1,0:T(1,128)S(1)} %get-tuple-element.32), channel_id=1, source_target_pairs={{0,8},{8,16},{16,24},{24,32},{32,40},{40,48},{48,56},{56,64},{64,7... | collective-permute-start | bytes 3080 | tf_op jit(solution)/shard_map/ppermute | solution.py:25
  751.3 8.5 %collective-permute-start.9 = (f32[1,256]{1,0:T(1,128)S(1)}, f32[1,256]{1,0:T(1,128)S(1)}, u32[]{:S(2)}, u32[]{:S(2)}) collective-permute-start(f32[1,256]{1,0:T(1,128)S(1)} %get-tuple-element.33), channel_id=1, source_target_pairs={{8,0},{16,8},{24,16},{32,24},{40,32},{48,40},{56,48},{64,56},{72,6... | collective-permute-start | bytes 3080 | tf_op jit(solution)/shard_map/ppermute | solution.py:28
  759.9 5.9 collective-permute-start.10
  761.8 7.8 collective-permute-start.11
  769.7 9.2 %collective-permute-start.12 = (f32[1,256]{1,0:T(1,128)S(1)}, f32[1,256]{1,0:T(1,128)S(1)}, u32[]{:S(2)}, u32[]{:S(2)}) collective-permute-start(f32[1,256]{1,0:T(1,128)S(1)} %get-tuple-element.30), channel_id=1, source_target_pairs={{0,8},{8,16},{16,24},{24,32},{32,40},{40,48},{48,56},{56,64},{64,7... | collective-permute-start | bytes 3080 | tf_op jit(solution)/shard_map/ppermute | solution.py:25
  771.7 8.5 %collective-permute-start.13 = (f32[1,256]{1,0:T(1,128)S(1)}, f32[1,256]{1,0:T(1,128)S(1)}, u32[]{:S(2)}, u32[]{:S(2)}) collective-permute-start(f32[1,256]{1,0:T(1,128)S(1)} %get-tuple-element.31), channel_id=1, source_target_pairs={{8,0},{16,8},{24,16},{32,24},{40,32},{48,40},{56,48},{64,56},{72,6... | collective-permute-start | bytes 3080 | tf_op jit(solution)/shard_map/ppermute | solution.py:28
  780.3 5.9 collective-permute-start.14
  782.2 7.8 collective-permute-start.15
  (7 other events, 71.6 us)
Sparse Core Ops, SparseCore 0:
  22.2 529.4 all-reduce.2
  675.8 39.5 reduce-scatter.3
